TPU v7x, 32 devices: a whole 2x2x4 slice. The times are simulated.
32 devices in a mesh: row: 2 (over x), col: 4 (over z), tok: 4 (over y, core).
Axes of the slice: x: 2, y: 2, z: 4, core: 2. Of those that a mesh axis runs over, the one named last changes fastest.
Arguments:
- activations: bfloat16 [4096, 2048], P(('row', 'col', 'tok')), may hold values from -6 to 6
- norm_gain: float32 [2048], replicated, may hold values from 0.1 to 1.9
- routes: int32 [4096, 8], P(('row', 'col', 'tok')), may hold values from 0 to 127, all different within a row; in each aligned block of 128 rows (0 to 127, 128 to 255, ...) at most 10 rows name the same one
- route_weights: float32 [4096, 8], P(('row', 'col', 'tok')), may hold values from 0.05 to 1
- gate_up_weight: bfloat16 [128, 2, 768, 2048], P(('row', 'col'), None, 'tok'), may hold values from -0.125 to 0.125
- down_weight: bfloat16 [128, 768, 2048], P(('row', 'col'), 'tok'), may hold values from -0.21875 to 0.21875
Outputs:
- expert_mix: bfloat16 [4096, 2048], P(('row', 'col', 'tok'))
Inputs may be any that keep to these rules, and one draw needn't show every extreme that they name: `routes`: within the rows of one device no expert is named by more than 10 rows, a bound that some block reaches.
All inputs are finite; a program needn't handle non-finite values.
Results may differ from a plain program's by a relative error of at most 0.0085.
Values may be sent and summed in bfloat16 or wider, within the bound.
No kernel may reach another device: no remote copies, remote signals or barrier semaphores. Data moves between devices by JAX's collectives and lax.ppermute only.
A program may use at most 384 MiB of HBM per device.

v0:
```python
import jax
import jax.numpy as jnp
from jax import lax
from jax.sharding import PartitionSpec as P

CAP = 10
EPSILON = 1e-06
ALL = ("row", "col", "tok")


def rank_in_block(block_routes, experts):
    onehot = (block_routes[:, None] == jnp.arange(experts, dtype=jnp.int32)[None, :]).astype(
        jnp.int32
    )
    before = jnp.cumsum(onehot, axis=0) - onehot
    return jnp.sum(before * onehot, axis=1)


def rms_normed(activations, norm_gain):
    values = activations.astype(jnp.float32)
    scale = lax.rsqrt(jnp.mean(values * values, axis=-1, keepdims=True) + EPSILON)
    return (values * scale * norm_gain).astype(jnp.bfloat16)


def local(activations, norm_gain, routes, route_weights, gate_up_weight, down_weight):
    count, features = activations.shape
    chosen = routes.shape[1]
    holding = gate_up_weight.shape[0]
    row_count = lax.axis_size("row")
    col_count = lax.axis_size("col")
    tok_count = lax.axis_size("tok")
    owners = row_count * col_count
    experts = holding * owners
    devices = owners * tok_count
    owner = lax.axis_index("row") * col_count + lax.axis_index("col")
    normed = rms_normed(activations, norm_gain)
    gates = route_weights / jnp.sum(route_weights, axis=1, keepdims=True)
    flat_routes = routes.reshape(-1)
    target = flat_routes * CAP + rank_in_block(flat_routes, experts)
    every_normed = lax.all_gather(normed, ALL, axis=0, tiled=True)
    every_target = lax.all_gather(target, ALL, axis=0, tiled=False)
    source = jnp.arange(devices, dtype=jnp.int32)[:, None]
    pair = jnp.arange(count * chosen, dtype=jnp.int32)[None, :]
    expert = every_target // CAP
    rank = every_target % CAP
    mine = expert // holding == owner
    slot = (
        (source % tok_count * owners + source // tok_count) * holding + expert % holding
    ) * CAP + rank
    slots = tok_count * owners * holding * CAP
    slot = jnp.where(mine, slot, slots)
    token = source * count + pair // chosen
    table = (
        jnp.full((slots,), devices * count, jnp.int32)
        .at[slot.reshape(-1)]
        .set(token.reshape(-1), mode="drop")
    )
    picked = jnp.take(every_normed, table, axis=0, mode="fill", fill_value=0)
    picked = picked.reshape(tok_count * owners, holding, CAP, features)
    both = jnp.einsum(
        "sjcd,jgfd->sjcgf", picked, gate_up_weight, preferred_element_type=jnp.float32
    )
    hidden = (jax.nn.silu(both[:, :, :, 0, :]) * both[:, :, :, 1, :]).astype(jnp.bfloat16)
    partial = jnp.einsum("sjcf,jfd->sjcd", hidden, down_weight, preferred_element_type=jnp.float32)
    summed = lax.psum_scatter(partial, "tok", scatter_dimension=0, tiled=True)
    results = summed.astype(jnp.bfloat16)
    returned = lax.all_to_all(results, ("row", "col"), split_axis=0, concat_axis=0, tiled=True)
    picked_back = jnp.take(returned.reshape(experts * CAP, features), target, axis=0)
    picked_back = picked_back.reshape(count, chosen, features)
    mixed = jnp.einsum("tk,tkd->td", gates, picked_back.astype(jnp.float32))
    return mixed.astype(jnp.bfloat16)


def solution(mesh):
    in_specs = (
        P(("row", "col", "tok"), None),
        P(),
        P(("row", "col", "tok"), None),
        P(("row", "col", "tok"), None),
        P(("row", "col"), None, "tok", None),
        P(("row", "col"), "tok", None),
    )
    out_specs = P(("row", "col", "tok"), None)
    return jax.shard_map(local, mesh=mesh, in_specs=in_specs, out_specs=out_specs, check_vma=False)
```

profile of v0, /device:TPU:0, one launch (start us, length us, event | category | flops | bytes accessed | tf_op | source)
XLA Modules:
  0.0 799.6 jit_solution(5752293919866283598)
XLA Ops:
  6.5 1.2 fusion.16
  7.8 2.0 fusion.18
  9.9 0.8 copy.47
  11.4 0.7 broadcast_multiply_fusion
  12.3 0.4 fusion.20
  12.7 44.2 %all-gather = s32[32,1,1024]{2,1,0:T(1,128)S(1)} all-gather(s32[1,1,1024]{2,1,0:T(1,128)S(1)} %add_bitcast_fusion.1), channel_id=1, replica_groups=mesh['row'=2,'col'=4,'tok'=4] {'row','col','tok'}, dimensions={0}, use_global_device_ids=true | all-gather | bytes 135168 | tf_op jit(solution)/shard_map/all_gather | solution.py:41
  56.9 0.3 broadcast_remainder_fusion
  57.9 120.3 %scatter_custom_fusion = s32[5120]{0:T(1024)S(1)} fusion(s32[32768]{0:T(1024)S(1)} %bitcast.89, s32[32768]{0:T(1024)S(1)} %bitcast.88, s32[]{:T(128)} %constant.127.clone.1), kind=kCustom, calls=%fused_computation.64 | custom fusion | bytes 20484 | tf_op jit(solution)/shard_map/scatter | solution.py:56
  178.2 0.3 broadcast_in_dim.41
  178.5 46.8 %gather_fusion = bf16[5120,2048]{1,0:T(8,128)(2,1)} fusion(bf16[4096,2048]{1,0:T(8,128)(2,1)} %all-gather.3.cloned.1.call-done, s32[5120]{0:T(1024)S(1)} %fusion.35), kind=kCustom, calls=%fused_computation | custom fusion | bytes 41963520 | tf_op jit(solution)/shard_map/jit(_take)/gather | solution.py:58
  225.3 34.0 %gather.13 = bf16[32,16,10,2048]{3,2,1,0:T(8,128)(2,1)} reshape(bf16[5120,2048]{1,0:T(8,128)(2,1)} %gather_fusion) | data formatting | bytes 41943040 | tf_op jit(solution)/shard_map/jit(_take)/gather | solution.py:58
  259.3 22.7 %select_bitcast_fusion = bf16[32,16,10,2048,1]{3,2,1,0,4:T(8,128)(2,1)} fusion(bf16[32,16,10,2048]{3,2,1,0:T(8,128)(2,1)} %gather.13, pred[32,16,10]{2,1,0:T(8,128)(4,1)S(1)} %broadcast_in_dim.41), kind=kLoop, calls=%fused_computation.3 | loop fusion | flops 10485760 | bytes 41948160 | tf_op jit(solution)/shard_map/jit(_take)/select_n | solution.py:58
  282.1 34.1 %fusion.8 = f32[32,16,10,2,192]{4,0,3,2,1:T(8,128)} fusion(bf16[16,2,192,2048]{3,2,1,0:T(8,128)(2,1)} %param.10, bf16[32,16,10,2048,1]{3,2,1,0,4:T(8,128)(2,1)} %select_bitcast_fusion), kind=kOutput, calls=%fused_computation.16 | convolution fusion | flops 8053063680 | bytes 54001664 | tf_op jit(solution)/shard_map/sjcd,jgfd->sjcgf/dot_general | solution.py:60
  316.2 22.9 %convolution_bitcast_fusion = f32[32,16,10,2048]{3,0,2,1:T(8,128)} fusion(bf16[16,192,2048]{2,1,0:T(8,128)(2,1)} %param.11, f32[32,16,10,2,192]{4,0,3,2,1:T(8,128)} %fusion.8), kind=kOutput, calls=%fused_computation.7 | convolution fusion | flops 4032430080 | bytes 62390272 | tf_op jit(solution)/shard_map/sjcf,jfd->sjcd/dot_general | solution.py:64
  339.0 285.4 %reduce-scatter.2.cloned.1.call-done = f32[8,16,10,2048]{3,0,2,1:T(8,128)} async-done(((f32[32,16,10,2048]{3,0,2,1:T(8,128)}), f32[8,16,10,2048]{3,0,2,1:T(8,128)}) %reduce-scatter.2.cloned.1.call-update) | async-done | bytes 10485776 | tf_op jit(solution)/shard_map/reduce_scatter | solution.py:65
  624.4 4.8 convert_element_type.28
  629.2 5.2 copy.59
  634.4 5.5 all-to-all-start
  640.5 116.0 %all-to-all-done = bf16[8,16,10,2048]{3,1,2,0:T(8,128)(2,1)} async-done(((bf16[8,16,10,2048]{3,1,2,0:T(8,128)(2,1)}), bf16[8,16,10,2048]{3,1,2,0:T(8,128)(2,1)}, u32[]{:S(2)}, u32[]{:S(2)}) %all-to-all-start) | async-done | bytes 5242912 | tf_op jit(solution)/shard_map/all_to_all | solution.py:67
  756.6 9.7 %copy.60 = bf16[8,16,10,2048]{3,2,1,0:T(8,128)(2,1)} copy(bf16[8,16,10,2048]{3,1,2,0:T(8,128)(2,1)} %all-to-all-done) | data formatting | bytes 10485760 | tf_op jit(solution)/shard_map/all_to_all | solution.py:67
  766.3 9.8 %reshape.243 = bf16[1280,2048]{1,0:T(8,128)(2,1)} reshape(bf16[8,16,10,2048]{3,2,1,0:T(8,128)(2,1)} %copy.60) | data formatting | bytes 10485760 | tf_op jit(solution)/shard_map/reshape | solution.py:68
  776.1 12.0 %gather_fusion.1 = bf16[1024,2048]{1,0:T(8,128)(2,1)} fusion(bf16[1280,2048]{1,0:T(8,128)(2,1)} %reshape.243, s32[1024]{0:T(1024)S(1)} %broadcast_clamp_fusion), kind=kCustom, calls=%fused_computation.1 | custom fusion | bytes 8392704 | tf_op jit(solution)/shard_map/jit(_take)/gather | solution.py:68
  788.1 3.5 fusion.6
  791.6 1.1 copy.82
  (50 shorter events, 2.2 us)
Async XLA Ops:
  6.5 172.0 %all-gather.3.cloned.1.call-start = ((), (), s32[]{:S(2)}) async-start(), calls=%async_computation.2 | async-start | bytes 17301504 | tf_op jit(solution)/shard_map/all_gather | solution.py:40
  9.8 614.6 %reduce-scatter.2.cloned.1.call-start = ((), (), s32[]{:S(2)}) async-start(), calls=%async_computation.3 | async-start | bytes 52428800 | tf_op jit(solution)/shard_map/reduce_scatter | solution.py:65
  12.2 213.1 %copy-start = (s32[128,8]{1,0:T(8,128)}, s32[128,8]{1,0:T(8,128)S(1)}, u32[]{:S(2)}) copy-start(s32[128,8]{1,0:T(8,128)S(1)} %copy.53) | copy-start | bytes 12292
  12.6 45.3 %copy-start.2 = (s32[1024]{0:T(1024)}, s32[1024]{0:T(1024)S(1)}, u32[]{:S(2)}) copy-start(s32[1024]{0:T(1024)S(1)} %fusion.20) | copy-start | bytes 12292
  629.2 10.7 %copy-start.1 = (s32[128,8]{1,0:T(8,128)S(1)}, s32[128,8]{1,0:T(8,128)}, u32[]{:S(2)}) copy-start(s32[128,8]{1,0:T(8,128)} %copy-done) | copy-start | bytes 12292
  629.2 10.8 %copy-start.3 = (s32[1024]{0:T(1024)S(1)}, s32[1024]{0:T(1024)}, u32[]{:S(2)}) copy-start(s32[1024]{0:T(1024)} %copy-done.2) | copy-start | bytes 12292
  629.2 11.0 %copy-start.4 = (s32[128,8]{0,1:T(8,128)S(1)}, s32[128,8]{0,1:T(8,128)}, u32[]{:S(2)}) copy-start(s32[128,8]{0,1:T(8,128)} %param.8) | copy-start | bytes 12292
  629.2 11.1 %copy-start.5 = (f32[128,8]{0,1:T(8,128)S(1)}, f32[128,8]{0,1:T(8,128)}, u32[]{:S(2)}) copy-start(f32[128,8]{0,1:T(8,128)} %param.9) | copy-start | bytes 12292
  634.4 122.1 %all-to-all-start = ((bf16[8,16,10,2048]{3,1,2,0:T(8,128)(2,1)}), bf16[8,16,10,2048]{3,1,2,0:T(8,128)(2,1)}, u32[]{:S(2)}, u32[]{:S(2)}) async-start(bf16[8,16,10,2048]{3,1,2,0:T(8,128)(2,1)} %copy.59), calls=%async_computation.1 | async-start | bytes 10485760 | tf_op jit(solution)/shard_map/all_to_all | solution.py:67
Sparse Core Ops, SparseCore 0:
  10.2 117.7 all-gather.2
  339.1 285.1 reduce-scatter.1
where the time goes:
time: 801 us; the launch traced here: 800 us
  waiting for transfers between devices  401 us (50%)
  local copies, waits for them, and re-layouts  241 us (30%)
  matrix products  60.4 us (8%)
  blocking collectives  44.2 us (6%)
  other arithmetic  33 us (4%)
  between operations  13.7 us (2%)
    reduce_scatter x1, waiting for transfers between devices, local(): summed = lax.psum_scatter(partial, 'tok', scatter_dimension=0, tiled=True)  285 us
    scatter x1, local copies, waits for them, and re-layouts, local(): table = jnp.full((slots,), devices * count, jnp.int32).at[slot.reshape(-1...  120 us
    all_to_all x1, waiting for transfers between devices, local(): lax.all_to_all(results, ('row', 'col'), split_axis=0, concat_axis=0, tile...  116 us
    gather x2, local copies, waits for them, and re-layouts, local(): picked = jnp.take(every_normed, table, axis=0, mode='fill', fill_value=0)  80.8 us
    all_gather x1, blocking collectives, local(): every_target = lax.all_gather(target, ALL, axis=0, tiled=False)  44.2 us
    dot_general x1, matrix products, local(): jnp.einsum('sjcd,jgfd->sjcgf', picked, gate_up_weight, preferred_element_...  34.1 us
    dot_general x1, matrix products, local(): jnp.einsum('sjcf,jfd->sjcd', hidden, down_weight, preferred_element_type=...  22.9 us
    select_n x1, other arithmetic, local(): picked = jnp.take(every_normed, table, axis=0, mode='fill', fill_value=0)  22.7 us
  transfers between devices with their start and end apart: 3, of which 2 were waited for; matrix products, arithmetic and copies ran while one was open for 16% of the time, Pallas kernels for 0%

commit v1 on v0

--- a/solution.py
+++ b/solution.py
@@ -6,6 +6,18 @@
 CAP = 10
 EPSILON = 1e-06
 ALL = ("row", "col", "tok")
+
+
+def exchange_directly(shard, axis, split, join):
+    ways, here = (lax.axis_size(axis), lax.axis_index(axis))
+    width = shard.shape[split] // ways
+    turned = jnp.roll(shard, -here * width, axis=split)
+    got = [lax.slice_in_dim(turned, 0, width, axis=split)]
+    for far in range(1, ways):
+        sent = lax.slice_in_dim(turned, far * width, (far + 1) * width, axis=split)
+        got.append(lax.ppermute(sent, axis, [(d, (d + far) % ways) for d in range(ways)]))
+    line = jnp.concatenate(got[::-1], axis=join)
+    return jnp.roll(line, (here + 1) * got[0].shape[join], axis=join)
 
 
 def rank_in_block(block_routes, experts):
@@ -64,7 +76,7 @@
     partial = jnp.einsum("sjcf,jfd->sjcd", hidden, down_weight, preferred_element_type=jnp.float32)
     summed = lax.psum_scatter(partial, "tok", scatter_dimension=0, tiled=True)
     results = summed.astype(jnp.bfloat16)
-    returned = lax.all_to_all(results, ("row", "col"), split_axis=0, concat_axis=0, tiled=True)
+    returned = exchange_directly(results, ("row", "col"), 0, 0)
     picked_back = jnp.take(returned.reshape(experts * CAP, features), target, axis=0)
     picked_back = picked_back.reshape(count, chosen, features)
     mixed = jnp.einsum("tk,tkd->td", gates, picked_back.astype(jnp.float32))

time: 801 us -> 855 us (1.067)
  local copies, waits for them, and re-layouts: 241 us -> 310 us
  waiting for transfers between devices: 401 us -> 363 us
  other arithmetic: 33 us -> 44.3 us
    all_to_all x1 -> x0, waiting for transfers between devices: 116 us -> none  [local(): lax.all_to_all(results, ('row', 'col'), split_axis=0, concat_axis=0, tile...]
    ppermute x0 -> x7, waiting for transfers between devices: none -> 77.1 us  [exchange_directly(): lax.ppermute(sent, axis, [(d, (d + far) % ways) for d in range(ways)])]
    slice x0 -> x8, local copies, waits for them, and re-layouts: none -> 28.1 us  [the longest x7 14.8 us: exchange_directly(): sent = lax.slice_in_dim(turned, far * width, (far + 1) * width, axis=split)]
    concatenate x0 -> x1, local copies, waits for them, and re-layouts: none -> 27.1 us  [exchange_directly(): line = jnp.concatenate(got[::-1], axis=join)]
    ppermute x0 -> x7, local copies, waits for them, and re-layouts: none -> 22 us  [exchange_directly(): lax.ppermute(sent, axis, [(d, (d + far) % ways) for d in range(ways)])]
    concatenate x0 -> x2, other arithmetic: none -> 11.3 us  [the longest x1 7.74 us: exchange_directly(): return jnp.roll(line, (here + 1) * got[0].shape[join], axis=join)]
    ppermute x0 -> x7, starting transfers between devices: none -> 10.9 us  [exchange_directly(): lax.ppermute(sent, axis, [(d, (d + far) % ways) for d in range(ways)])]
    all_to_all x1 -> x0, local copies, waits for them, and re-layouts: 9.73 us -> none  [local(): lax.all_to_all(results, ('row', 'col'), split_axis=0, concat_axis=0, tile...]
  transfers between devices with their start and end apart: 3 -> 9, of which waited for: 2 -> 3; matrix products, arithmetic and copies ran while one was open for 16% -> 19% of each run, Pallas kernels for 0% -> 0%
where the time goes in v1:
time: 855 us; the launch traced here: 847 us
  waiting for transfers between devices  363 us (42%)
  local copies, waits for them, and re-layouts  310 us (36%)
  matrix products  60.6 us (7%)
  other arithmetic  44.3 us (5%)
  blocking collectives  44.1 us (5%)
  between operations  14 us (2%)
  starting transfers between devices  11 us (1%)
    reduce_scatter x1, waiting for transfers between devices, local(): summed = lax.psum_scatter(partial, 'tok', scatter_dimension=0, tiled=True)  285 us
    scatter x1, local copies, waits for them, and re-layouts, local(): table = jnp.full((slots,), devices * count, jnp.int32).at[slot.reshape(-1...  121 us
    gather x2, local copies, waits for them, and re-layouts, local(): picked = jnp.take(every_normed, table, axis=0, mode='fill', fill_value=0)  80.8 us
    ppermute x7, waiting for transfers between devices, exchange_directly(): lax.ppermute(sent, axis, [(d, (d + far) % ways) for d in range(ways)])  77.1 us
    all_gather x1, blocking collectives, local(): every_target = lax.all_gather(target, ALL, axis=0, tiled=False)  44.1 us
    dot_general x1, matrix products, local(): jnp.einsum('sjcd,jgfd->sjcgf', picked, gate_up_weight, preferred_element_...  34.1 us
    concatenate x1, local copies, waits for them, and re-layouts, exchange_directly(): line = jnp.concatenate(got[::-1], axis=join)  27.1 us
    dot_general x1, matrix products, local(): jnp.einsum('sjcf,jfd->sjcd', hidden, down_weight, preferred_element_type=...  23 us
  transfers between devices with their start and end apart: 9, of which 3 were waited for; matrix products, arithmetic and copies ran while one was open for 19% of the time, Pallas kernels for 0%

profile of v1, /device:TPU:0, one launch (start us, length us, event | category | flops | bytes accessed | tf_op | source)
XLA Modules:
  0.0 847.0 jit_solution(10397194664405446235)
XLA Ops:
  12.7 44.1 %all-gather = s32[32,1,1024]{2,1,0:T(1,128)S(1)} all-gather(s32[1,1,1024]{2,1,0:T(1,128)S(1)} %add_bitcast_fusion.1), channel_id=1, replica_groups=mesh['row'=2,'col'=4,'tok'=4] {'row','col','tok'}, dimensions={0}, use_global_device_ids=true | all-gather | bytes 135168 | tf_op jit(solution)/shard_map/all_gather | solution.py:53
  57.8 120.6 %scatter_custom_fusion = s32[5120]{0:T(1024)S(1)} fusion(s32[32768]{0:T(1024)S(1)} %bitcast.89, s32[32768]{0:T(1024)S(1)} %bitcast.88, s32[]{:T(128)} %constant.145.clone.1), kind=kCustom, calls=%fused_computation.70 | custom fusion | bytes 20484 | tf_op jit(solution)/shard_map/scatter | solution.py:68
  178.7 46.8 %gather_fusion = bf16[5120,2048]{1,0:T(8,128)(2,1)} fusion(bf16[4096,2048]{1,0:T(8,128)(2,1)} %all-gather.3.cloned.1.call-done, s32[5120]{0:T(1024)S(1)} %fusion.37), kind=kCustom, calls=%fused_computation | custom fusion | bytes 41963520 | tf_op jit(solution)/shard_map/jit(_take)/gather | solution.py:70
  225.5 34.0 %gather.13 = bf16[32,16,10,2048]{3,2,1,0:T(8,128)(2,1)} reshape(bf16[5120,2048]{1,0:T(8,128)(2,1)} %gather_fusion) | data formatting | bytes 41943040 | tf_op jit(solution)/shard_map/jit(_take)/gather | solution.py:70
  259.5 22.7 %select_bitcast_fusion = bf16[32,16,10,2048,1]{3,2,1,0,4:T(8,128)(2,1)} fusion(bf16[32,16,10,2048]{3,2,1,0:T(8,128)(2,1)} %gather.13, pred[32,16,10]{2,1,0:T(8,128)(4,1)S(1)} %broadcast_in_dim.41), kind=kLoop, calls=%fused_computation.3 | loop fusion | flops 10485760 | bytes 41948160 | tf_op jit(solution)/shard_map/jit(_take)/select_n | solution.py:70
  282.3 34.1 %fusion.10 = f32[32,16,10,2,192]{4,0,3,2,1:T(8,128)} fusion(bf16[16,2,192,2048]{3,2,1,0:T(8,128)(2,1)} %param.12, bf16[32,16,10,2048,1]{3,2,1,0,4:T(8,128)(2,1)} %select_bitcast_fusion), kind=kOutput, calls=%fused_computation.22 | convolution fusion | flops 8053063680 | bytes 54001664 | tf_op jit(solution)/shard_map/sjcd,jgfd->sjcgf/dot_general | solution.py:72
  316.3 23.0 %convolution_bitcast_fusion = f32[32,16,10,2048]{3,0,2,1:T(8,128)} fusion(bf16[16,192,2048]{2,1,0:T(8,128)(2,1)} %param.13, f32[32,16,10,2,192]{4,0,3,2,1:T(8,128)} %fusion.10), kind=kOutput, calls=%fused_computation.7 | convolution fusion | flops 4032430080 | bytes 62390272 | tf_op jit(solution)/shard_map/sjcf,jfd->sjcd/dot_general | solution.py:76
  339.4 285.4 %reduce-scatter.2.cloned.1.call-done = f32[8,16,10,2048]{3,0,2,1:T(8,128)} async-done(((f32[32,16,10,2048]{3,0,2,1:T(8,128)}), f32[8,16,10,2048]{3,0,2,1:T(8,128)}) %reduce-scatter.2.cloned.1.call-update) | async-done | bytes 10485776 | tf_op jit(solution)/shard_map/reduce_scatter | solution.py:77
  624.8 4.8 convert_element_type.28
  629.6 3.6 fusion.5
  633.2 13.3 %fusion.48 = (bf16[1,16,10,2048]{3,0,2,1:T(2,128)(2,1)}, bf16[1,16,10,2048]{3,0,2,1:T(2,128)(2,1)S(1)}, bf16[1,16,10,2048]{3,0,2,1:T(2,128)(2,1)S(1)}, bf16[1,16...) fusion(bf16[8,16,10,2048]{3,0,2,1:T(8,128)(2,1)S(1)} %fusion.5), kind=kLoop, calls=%fused_computation.97 | loop fusion | bytes 10485760 | tf_op jit(solution)/shard_map/slice | solution.py:15
  648.1 4.4 collective-permute-start
  672.8 37.7 %collective-permute-done.1 = bf16[1,16,10,2048]{3,1,2,0:T(8,128)(2,1)} collective-permute-done((bf16[1,16,10,2048]{3,1,2,0:T(8,128)(2,1)}, bf16[1,16,10,2048]{3,1,2,0:T(8,128)(2,1)}, u32[]{:S(2)}, u32[]{:S(2)}) %collective-permute-start.1) | collective-permute-done | bytes 655392 | tf_op jit(solution)/shard_map/ppermute | solution.py:18
  711.9 3.5 copy.69
  715.3 3.5 copy.70
  718.9 3.5 copy.71
  725.8 39.4 %collective-permute-done.5 = bf16[1,16,10,2048]{3,1,2,0:T(8,128)(2,1)} collective-permute-done((bf16[1,16,10,2048]{3,1,2,0:T(8,128)(2,1)}, bf16[1,16,10,2048]{3,1,2,0:T(8,128)(2,1)}, u32[]{:S(2)}, u32[]{:S(2)}) %collective-permute-start.5) | collective-permute-done | bytes 655392 | tf_op jit(solution)/shard_map/ppermute | solution.py:18
  768.6 3.5 copy.74
  772.1 27.1 %concatenate.6 = bf16[8,16,10,2048]{3,0,2,1:T(8,128)(2,1)} concatenate(bf16[1,16,10,2048]{3,0,2,1:T(2,128)(2,1)S(1)} %copy.68, bf16[1,16,10,2048]{3,0,2,1:T(2,128)(2,1)} %copy.69, bf16[1,16,10,2048]{3,0,2,1:T(2,128)(2,1)} %copy.70, bf16[1,16,10,2048]{3,0,2,1:T(2,128)(2,1)} %copy.71, bf16[1,16,10,2048]{3,0,2,1:T(2,128)(2,1)} %copy.72, bf16[1,16,10,2048]{3,0,2,1:T(2,128)(2,1)} %copy.73, ...), dimensions={0} | concatenate | bytes 10485760 | tf_op jit(solution)/shard_map/concatenate | solution.py:19
  799.2 7.7 fusion.4
  807.0 6.5 copy.75
  813.5 9.8 %reshape.243 = bf16[1280,2048]{1,0:T(8,128)(2,1)} reshape(bf16[8,16,10,2048]{3,2,1,0:T(8,128)(2,1)} %copy.75) | data formatting | bytes 10485760 | tf_op jit(solution)/shard_map/reshape | solution.py:80
  823.3 12.0 %gather_fusion.1 = bf16[1024,2048]{1,0:T(8,128)(2,1)} fusion(bf16[1280,2048]{1,0:T(8,128)(2,1)} %reshape.243, s32[1024]{0:T(1024)S(1)} %broadcast_clamp_fusion), kind=kCustom, calls=%fused_computation.1 | custom fusion | bytes 8392704 | tf_op jit(solution)/shard_map/jit(_take)/gather | solution.py:80
  835.3 3.5 fusion.8
  (81 shorter events, 38.5 us)
Async XLA Ops:
  6.5 172.2 %all-gather.3.cloned.1.call-start = ((), (), s32[]{:S(2)}) async-start(), calls=%async_computation.1 | async-start | bytes 17301504 | tf_op jit(solution)/shard_map/all_gather | solution.py:52
  9.8 615.0 %reduce-scatter.2.cloned.1.call-start = ((), (), s32[]{:S(2)}) async-start(), calls=%async_computation.2 | async-start | bytes 52428800 | tf_op jit(solution)/shard_map/reduce_scatter | solution.py:77
  12.2 213.3 %copy-start.1 = (s32[128,8]{1,0:T(8,128)}, s32[128,8]{1,0:T(8,128)S(1)}, u32[]{:S(2)}) copy-start(s32[128,8]{1,0:T(8,128)S(1)} %copy.55) | copy-start | bytes 12292
  12.6 45.2 %copy-start.3 = (s32[1024]{0:T(1024)}, s32[1024]{0:T(1024)S(1)}, u32[]{:S(2)}) copy-start(s32[1024]{0:T(1024)S(1)} %fusion.22) | copy-start | bytes 12292
  633.2 20.8 %copy-start.2 = (s32[128,8]{1,0:T(8,128)S(1)}, s32[128,8]{1,0:T(8,128)}, u32[]{:S(2)}) copy-start(s32[128,8]{1,0:T(8,128)} %copy-done.1) | copy-start | bytes 12292
  633.2 20.9 %copy-start.4 = (s32[1024]{0:T(1024)S(1)}, s32[1024]{0:T(1024)}, u32[]{:S(2)}) copy-start(s32[1024]{0:T(1024)} %copy-done.3) | copy-start | bytes 12292
  633.2 21.1 %copy-start.5 = (s32[128,8]{0,1:T(8,128)S(1)}, s32[128,8]{0,1:T(8,128)}, u32[]{:S(2)}) copy-start(s32[128,8]{0,1:T(8,128)} %param.10) | copy-start | bytes 12292
  633.2 21.2 %copy-start.6 = (f32[128,8]{0,1:T(8,128)S(1)}, f32[128,8]{0,1:T(8,128)}, u32[]{:S(2)}) copy-start(f32[128,8]{0,1:T(8,128)} %param.11) | copy-start | bytes 12292
  648.1 22.6 %collective-permute-start = (bf16[1,16,10,2048]{3,1,2,0:T(8,128)(2,1)}, bf16[1,16,10,2048]{3,1,2,0:T(8,128)(2,1)S(1)}, u32[]{:S(2)}, u32[]{:S(2)}) collective-permute-start(bf16[1,16,10,2048]{3,1,2,0:T(8,128)(2,1)} %copy.61), channel_id=1, source_target_pairs={{0,28},{4,0},{8,4},{12,8},{16,12},{20,16},{24,20},{28,24},{1,29},{... | collective-permute-start | bytes 1966088 | tf_op jit(solution)/shard_map/ppermute | solution.py:18
  654.0 56.4 %collective-permute-start.1 = (bf16[1,16,10,2048]{3,1,2,0:T(8,128)(2,1)}, bf16[1,16,10,2048]{3,1,2,0:T(8,128)(2,1)}, u32[]{:S(2)}, u32[]{:S(2)}) collective-permute-start(bf16[1,16,10,2048]{3,1,2,0:T(8,128)(2,1)} %copy.62), channel_id=1, source_target_pairs={{0,24},{4,28},{8,0},{12,4},{16,8},{20,12},{24,16},{28,20},{1,25},{... | collective-permute-start | bytes 1966088 | tf_op jit(solution)/shard_map/ppermute | solution.py:18
  657.3 58.0 %collective-permute-start.2 = (bf16[1,16,10,2048]{3,1,2,0:T(8,128)(2,1)}, bf16[1,16,10,2048]{3,1,2,0:T(8,128)(2,1)}, u32[]{:S(2)}, u32[]{:S(2)}) collective-permute-start(bf16[1,16,10,2048]{3,1,2,0:T(8,128)(2,1)} %copy.63), channel_id=1, source_target_pairs={{0,20},{4,24},{8,28},{12,0},{16,4},{20,8},{24,12},{28,16},{1,21},{... | collective-permute-start | bytes 1966088 | tf_op jit(solution)/shard_map/ppermute | solution.py:18
  661.3 57.6 %collective-permute-start.3 = (bf16[1,16,10,2048]{3,1,2,0:T(8,128)(2,1)}, bf16[1,16,10,2048]{3,1,2,0:T(8,128)(2,1)}, u32[]{:S(2)}, u32[]{:S(2)}) collective-permute-start(bf16[1,16,10,2048]{3,1,2,0:T(8,128)(2,1)} %copy.64), channel_id=1, source_target_pairs={{0,16},{4,20},{8,24},{12,28},{16,0},{20,4},{24,8},{28,12},{1,17},{... | collective-permute-start | bytes 1966088 | tf_op jit(solution)/shard_map/ppermute | solution.py:18
  665.6 56.7 %collective-permute-start.4 = (bf16[1,16,10,2048]{3,1,2,0:T(8,128)(2,1)}, bf16[1,16,10,2048]{3,1,2,0:T(8,128)(2,1)}, u32[]{:S(2)}, u32[]{:S(2)}) collective-permute-start(bf16[1,16,10,2048]{3,1,2,0:T(8,128)(2,1)} %copy.65), channel_id=1, source_target_pairs={{0,12},{4,16},{8,20},{12,24},{16,28},{20,0},{24,4},{28,8},{1,13},{... | collective-permute-start | bytes 1966088 | tf_op jit(solution)/shard_map/ppermute | solution.py:18
  670.7 94.5 %collective-permute-start.5 = (bf16[1,16,10,2048]{3,1,2,0:T(8,128)(2,1)}, bf16[1,16,10,2048]{3,1,2,0:T(8,128)(2,1)}, u32[]{:S(2)}, u32[]{:S(2)}) collective-permute-start(bf16[1,16,10,2048]{3,1,2,0:T(8,128)(2,1)} %copy.66), channel_id=1, source_target_pairs={{0,8},{4,12},{8,16},{12,20},{16,24},{20,28},{24,0},{28,4},{1,9},{5... | collective-permute-start | bytes 1966088 | tf_op jit(solution)/shard_map/ppermute | solution.py:18
  710.4 58.2 %collective-permute-start.6 = (bf16[1,16,10,2048]{3,1,2,0:T(8,128)(2,1)}, bf16[1,16,10,2048]{3,1,2,0:T(8,128)(2,1)}, u32[]{:S(2)}, u32[]{:S(2)}) collective-permute-start(bf16[1,16,10,2048]{3,1,2,0:T(8,128)(2,1)} %copy.67), channel_id=1, source_target_pairs={{0,4},{4,8},{8,12},{12,16},{16,20},{20,24},{24,28},{28,0},{1,5},{5... | collective-permute-start | bytes 1966088 | tf_op jit(solution)/shard_map/ppermute | solution.py:18
  715.3 56.8 %copy-start = (bf16[1,16,10,2048]{3,0,2,1:T(2,128)(2,1)S(1)}, bf16[1,16,10,2048]{3,0,2,1:T(2,128)(2,1)}, u32[]{:S(2)}) copy-start(bf16[1,16,10,2048]{3,0,2,1:T(2,128)(2,1)} %get-tuple-element.6) | copy-start | bytes 1966084
Sparse Core Ops, SparseCore 0:
  10.2 117.7 all-gather.2
  339.5 285.2 reduce-scatter.1
